TPU v7x, 32 devices: a whole 2x2x4 slice. The times are simulated.
32 devices in a mesh: grp: 4 (over x, core), rel: 8 (over z, y).
Axes of the slice: x: 2, y: 2, z: 4, core: 2. Of those that a mesh axis runs over, the one named last changes fastest.
Arguments:
- head_ids: int32 [65536], P(('grp', 'rel')), may hold values from 0 to 1023
- relations: int32 [65536, 1], P(('grp', 'rel')), may hold values from 0 to 31; in each aligned block of 2048 rows (0 to 2047, 2048 to 4095, ...) at most 128 rows name the same one
- tail_ids: int32 [65536], P(('grp', 'rel')), may hold values from 0 to 1023
- neg_owner: int32 [1], replicated, may hold values from 0 to 31
- entities: bfloat16 [32768, 512], P(('grp', 'rel')), may hold values from -0.3984375 to 0.3984375
- rel_weight: float32 [32, 512, 512], P('rel'), may hold values from -6 to 6
- rel_accum: float32 [32, 512], P('rel'), may hold values from 0.001 to 0.1
Outputs:
- losses: bfloat16 [65536], P(('grp', 'rel'))
- head_grad: bfloat16 [65536, 512], P(('grp', 'rel'))
- new_rel: float32 [32, 512, 512], P('rel')
- new_accum: float32 [32, 512], P('rel')
Inputs may be any that keep to these rules, and one draw needn't show every extreme that they name: `head_ids`: a row of the device's own shard of 1024 entity rows. `tail_ids`: a row of the device's own shard of 1024 entity rows. `relations`: in the 2048 rows of one device no relation is named by more than 128 rows; some relation is named by exactly 128. `neg_owner`: a device index, counted grp first, then rel.
All inputs are finite; a program needn't handle non-finite values.
Results may differ from a plain program's by a relative error of at most 0.0095.
Values may be sent and summed in bfloat16 or wider, within the bound.
No kernel may reach another device: no remote copies, remote signals or barrier semaphores. Data moves between devices by JAX's collectives and lax.ppermute only.
A program may use at most 128 MiB of HBM per device.

v0:
```python
import jax
import jax.numpy as jnp
from jax import lax
from jax.sharding import PartitionSpec as P

LEARNING_RATE = 1.0


def broadcast(shard, axis, root):
    mine = lax.axis_index(axis) == root
    return lax.psum(jnp.where(mine, shard, jnp.zeros_like(shard)), axis)


def score_rows(query_rows, tail_rows, negatives):
    positive = jnp.sum(query_rows.astype(jnp.float32) * tail_rows.astype(jnp.float32), axis=-1)
    neg_scores = jnp.dot(query_rows, negatives.T, preferred_element_type=jnp.float32)
    losses = jax.nn.softplus(-positive) + jnp.mean(jax.nn.softplus(neg_scores), axis=-1)
    coefs = (jax.nn.sigmoid(neg_scores) / negatives.shape[0]).astype(jnp.bfloat16)
    grad_query = -jax.nn.sigmoid(-positive)[:, None] * tail_rows.astype(jnp.float32)
    grad_query = grad_query + jnp.dot(coefs, negatives, preferred_element_type=jnp.float32)
    return (losses.astype(jnp.bfloat16), grad_query.astype(jnp.bfloat16))


def adagrad(weight, accumulator, gradient):
    new_accum = accumulator + jnp.mean(gradient * gradient, axis=-1)
    return (weight - LEARNING_RATE * gradient / jnp.sqrt(new_accum)[..., None], new_accum)


def one_hot(ids, count):
    return (ids[:, None] == jnp.arange(count, dtype=jnp.int32)[None, :]).astype(jnp.bfloat16)


def select_rows(selector, rows):
    return jnp.dot(selector, rows, preferred_element_type=jnp.float32).astype(jnp.bfloat16)


def per_device(head_ids, relations, tail_ids, neg_owner, entities, rel_weight, rel_accum):
    rows_here = head_ids.shape[0]
    width = entities.shape[1]
    shard_rows = entities.shape[0]
    owner_count = lax.axis_size("rel")
    local_rels = rel_weight.shape[0]
    rel_count = owner_count * local_rels
    capacity = 2 * rows_here // rel_count
    layout = (owner_count, local_rels, capacity)
    slots = rel_count * capacity
    negatives = broadcast(entities, ("grp", "rel"), neg_owner[0])
    rel_ids = relations[:, 0]
    rel_hot = one_hot(rel_ids, rel_count)
    order = jnp.arange(rows_here, dtype=jnp.int32)
    lower = (order[:, None] >= order[None, :]).astype(jnp.bfloat16)
    running = jnp.dot(lower, rel_hot, preferred_element_type=jnp.float32)
    rank = jnp.sum(running * rel_hot.astype(jnp.float32), axis=-1).astype(jnp.int32) - 1
    position = rel_ids * capacity + rank
    ids = jnp.stack([head_ids, tail_ids], axis=-1) + 1
    slot_ids = jnp.zeros((slots, 2), jnp.int32).at[position].set(ids) - 1
    held_rows = select_rows(one_hot(slot_ids[:, 0], shard_rows), entities).reshape(
        layout + (width,)
    )
    held_rows = lax.all_to_all(held_rows, "rel", split_axis=0, concat_axis=0, tiled=True)
    tail_send = select_rows(one_hot(slot_ids[:, 1], shard_rows), entities).reshape(
        layout + (width,)
    )
    held_tails = lax.all_to_all(tail_send, "rel", split_axis=0, concat_axis=0, tiled=True)
    matrices = rel_weight.astype(jnp.bfloat16)
    projected = jnp.einsum(
        "srcd,rde->srce", held_rows, matrices, preferred_element_type=jnp.float32
    ).astype(jnp.bfloat16)
    slot_losses, slot_grads = score_rows(
        projected.reshape(-1, width), held_tails.reshape(-1, width), negatives
    )
    grad_rows = slot_grads.reshape(held_rows.shape)
    partial_value = jnp.einsum(
        "srcd,srce->rde", held_rows, grad_rows, preferred_element_type=jnp.float32
    )
    summed = lax.psum(partial_value.astype(jnp.bfloat16), "grp").astype(jnp.float32)
    head_back = jnp.einsum(
        "srce,rde->srcd", grad_rows, matrices, preferred_element_type=jnp.float32
    ).astype(jnp.bfloat16)
    per_owner = local_rels * capacity
    extra = -(-per_owner // width)
    loss_rows = slot_losses.reshape(owner_count, per_owner)
    loss_rows = jnp.pad(loss_rows, ((0, 0), (0, extra * width - per_owner)))
    loss_rows = loss_rows.reshape(owner_count, extra, width)
    packed = jnp.concatenate([head_back.reshape(owner_count, per_owner, width), loss_rows], axis=1)
    packed = lax.all_to_all(packed, "rel", split_axis=0, concat_axis=0, tiled=True)
    back_grads = packed[:, :per_owner].reshape(slots, width)
    back_losses = packed[:, per_owner:].reshape(owner_count, extra * width)
    back_losses = back_losses[:, :per_owner].reshape(slots)
    taken = one_hot(position, slots)
    head_grad = select_rows(taken, back_grads)
    losses = jnp.dot(taken, back_losses, preferred_element_type=jnp.float32).astype(jnp.bfloat16)
    new_rel, new_accum = adagrad(rel_weight, rel_accum, summed)
    return (losses, head_grad, new_rel, new_accum)


def solution(mesh):
    placed = (
        P(("grp", "rel")),
        P(("grp", "rel"), None),
        P(("grp", "rel")),
        P(),
        P(("grp", "rel"), None),
        P("rel", None, None),
        P("rel", None),
    )
    return jax.shard_map(
        per_device,
        mesh=mesh,
        in_specs=placed,
        out_specs=(
            P(("grp", "rel")),
            P(("grp", "rel"), None),
            P("rel", None, None),
            P("rel", None),
        ),
        check_vma=False,
    )
```

profile of v0, /device:TPU:0, one launch (start us, length us, event | category | flops | bytes accessed | tf_op | source)
XLA Modules:
  0.0 491.5 jit_solution(8501658927828690532)
XLA Ops:
  7.2 2.3 fusion.29
  9.9 6.1 %scatter_custom_fusion = s32[4096,2]{1,0:T(8,128)S(1)} fusion(s32[2048]{0:T(1024)S(1)} %bitcast.78, s32[2048,2]{1,0:T(8,128)S(1)} %copy.56, s32[]{:T(128)} %constant.17.clone.1), kind=kCustom, calls=%fused_computation.47 | custom fusion | bytes 32772 | tf_op jit(solution)/shard_map/scatter | solution.py:56
  16.2 1.7 slice_reduce_fusion
  17.9 6.2 %fusion.13 = bf16[4096,512]{1,0:T(8,128)(2,1)} fusion(bf16[1024,512]{1,0:T(8,128)(2,1)S(1)} %copy-done.2, s32[4096]{0:T(1024)S(1)} %get-tuple-element.4), kind=kOutput, calls=%fused_computation.22 | convolution fusion | flops 4301258752 | bytes 5259264 | tf_op jit(solution)/shard_map/dot_general | solution.py:34
  24.2 7.3 %all-to-all-start.1 = ((bf16[8,4,128,512]{3,2,1,0:T(8,128)(2,1)}), bf16[8,4,128,512]{3,2,1,0:T(8,128)(2,1)}, u32[]{:S(2)}, u32[]{:S(2)}) async-start(bf16[8,4,128,512]{3,2,1,0:T(8,128)(2,1)} %bitcast.67), calls=%async_computation.1 | async-start | bytes 8388608 | tf_op jit(solution)/shard_map/all_to_all | solution.py:64
  31.5 6.2 %fusion.14 = bf16[4096,512]{1,0:T(8,128)(2,1)} fusion(bf16[1024,512]{1,0:T(8,128)(2,1)S(1)} %copy-done.2, s32[4096]{0:T(1024)S(1)} %get-tuple-element.5), kind=kOutput, calls=%fused_computation.23 | convolution fusion | flops 4301258752 | bytes 5259264 | tf_op jit(solution)/shard_map/dot_general | solution.py:34
  37.7 87.0 %all-to-all-done.1 = bf16[8,4,128,512]{3,2,1,0:T(8,128)(2,1)} async-done(((bf16[8,4,128,512]{3,2,1,0:T(8,128)(2,1)}), bf16[8,4,128,512]{3,2,1,0:T(8,128)(2,1)}, u32[]{:S(2)}, u32[]{:S(2)}) %all-to-all-start.1) | async-done | bytes 4194336 | tf_op jit(solution)/shard_map/all_to_all | solution.py:64
  124.8 4.6 all-to-all-start
  129.4 10.9 %all-reduce.3.cloned.1.call-start = ((), (), s32[]{:S(2)}) async-start(), calls=%async_computation.3 | async-start | bytes 2097152 | tf_op jit(solution)/shard_map/psum | solution.py:11
  140.9 1.0 broadcast_select_fusion
  142.0 84.8 %all-to-all-done = bf16[8,4,128,512]{3,2,1,0:T(8,128)(2,1)} async-done(((bf16[8,4,128,512]{3,2,1,0:T(8,128)(2,1)}), bf16[8,4,128,512]{3,2,1,0:T(8,128)(2,1)}, u32[]{:S(2)}, u32[]{:S(2)}) %all-to-all-start) | async-done | bytes 4194336 | tf_op jit(solution)/shard_map/all_to_all | solution.py:60
  226.8 7.2 %multiply_reduce_fusion = (f32[8,4,128]{2,0,1:T(8,128)S(1)}, bf16[8,4,128,512]{3,2,0,1:T(8,128)(2,1)S(1)}) fusion(bf16[8,4,128,512]{3,2,1,0:T(8,128)(2,1)} %all-to-all-done.1, f32[4,512,512]{2,1,0:T(8,128)} %param.12, bf16[8,4,128,512]{3,2,1,0:T(8,128)(2,1)} %all-to-all-done), kind=kOutput, calls=%fused_computation.18 | convolution fusion | flops 2159013888 | bytes 16793600 | tf_op jit(solution)/shard_map/srcd,rde->srce/dot_general | solution.py:66
  234.0 2.5 copy.61
  236.5 3.4 copy_convert_fusion
  239.9 4.2 copy.60
  244.1 82.8 %all-reduce.3.cloned.1.call-done = bf16[1024,512]{1,0:T(8,128)(2,1)} async-done(((bf16[1024,512]{1,0:T(8,128)(2,1)}), bf16[1024,512]{1,0:T(8,128)(2,1)}) %all-reduce.3.cloned.1.call-update) | async-done | bytes 1048592 | tf_op jit(solution)/shard_map/psum | solution.py:11
  326.9 16.2 %fusion.2 = (f32[4096]{0:T(1024)S(1)}, f32[4096,1024]{0,1:T(8,128)}) fusion(bf16[4096,512]{1,0:T(8,128)(2,1)} %bitcast.66, bf16[1024,512]{1,0:T(8,128)(2,1)} %all-reduce.3.cloned.1.call-done), kind=kOutput, calls=%fused_computation.5 | convolution fusion | flops 4324323328 | bytes 22036480 | tf_op jit(solution)/shard_map/dot_general | solution.py:16
  343.1 10.8 %fusion.9 = bf16[4096,512]{1,0:T(8,128)(2,1)} fusion(f32[8,4,128,512]{3,2,1,0:T(8,128)S(1)} %copy-done, bf16[1024,512]{1,0:T(8,128)(2,1)S(1)} %copy-done.7, f32[4096,1024]{0,1:T(8,128)} %get-tuple-element.11, f32[4096]{0:T(1024)S(1)} %bitcast.70), kind=kOutput, calls=%fused_computation.17 | convolution fusion | flops 4322230272 | bytes 30425088 | tf_op jit(solution)/shard_map/dot_general | solution.py:20
  354.0 4.6 convert_bitcast_fusion
  358.6 2.2 copy.63
  360.9 4.6 pad_maximum_fusion
  365.5 4.6 all-to-all-start.2
  370.3 7.2 %bitcast_convert_fusion = bf16[4,512,512]{2,1,0:T(8,128)(2,1)} fusion(bf16[8,4,128,512]{3,2,1,0:T(8,128)(2,1)} %all-to-all-done, bf16[8,4,128,512]{3,2,1,0:T(8,128)(2,1)} %bitcast.80), kind=kOutput, calls=%fused_computation.29 | convolution fusion | flops 2148532224 | bytes 10485760 | tf_op jit(solution)/shard_map/srcd,srce->rde/dot_general | solution.py:73
  377.5 52.6 %all-reduce.5.cloned.1.call-done = bf16[4,512,512]{2,1,0:T(8,128)(2,1)} async-done(((bf16[4,512,512]{2,1,0:T(8,128)(2,1)}), bf16[4,512,512]{2,1,0:T(8,128)(2,1)}) %all-reduce.5.cloned.1.call-update) | async-done | bytes 2097168 | tf_op jit(solution)/shard_map/psum | solution.py:76
  430.1 2.1 fusion.15
  432.8 5.5 %fusion.16 = f32[4,512,512]{2,1,0:T(8,128)} fusion(f32[4,512,512]{2,1,0:T(8,128)} %param.12, bf16[4,512,512]{2,1,0:T(8,128)(2,1)} %all-reduce.5.cloned.1.call-done, f32[4,512]{1,0:T(4,128)S(1)} %get-tuple-element.6), kind=kLoop, calls=%fused_computation.28 | loop fusion | flops 3145728 | bytes 10493952 | tf_op jit(solution)/shard_map/sub | solution.py:26
  438.3 25.8 %all-to-all-done.2 = bf16[8,513,512]{2,1,0:T(8,128)(2,1)} async-done(((bf16[8,513,512]{2,1,0:T(8,128)(2,1)}), bf16[8,513,512]{2,1,0:T(8,128)(2,1)}, u32[]{:S(2)}, u32[]{:S(2)}) %all-to-all-start.2) | async-done | bytes 4202528 | tf_op jit(solution)/shard_map/all_to_all | solution.py:86
  464.0 2.5 slice.19
  466.5 10.1 %fusion.21 = bf16[2048,512]{1,0:T(8,128)(2,1)} fusion(bf16[4096,512]{1,0:T(8,128)(2,1)S(1)} %bitcast.68, s32[2048]{0:T(1024)S(1)} %bitcast.76), kind=kOutput, calls=%fused_computation.37 | convolution fusion | flops 8599371776 | bytes 6299648 | tf_op jit(solution)/shard_map/dot_general | solution.py:34
  476.6 0.8 slice.18
  477.4 6.2 %fusion.1 = f32[1,2048]{1,0:T(1,128)S(1)} fusion(bf16[4096,1]{0,1:T(2,128)(2,1)S(1)} %bitcast.71, s32[2048]{0:T(1024)S(1)} %bitcast.77), kind=kOutput, calls=%fused_computation.4 | convolution fusion | flops 25165824 | bytes 24576 | tf_op jit(solution)/shard_map/dot_general | solution.py:92
  483.7 0.6 convert_element_type.102
  (31 shorter events, 1.5 us)
Async XLA Ops:
  7.2 2.3 copy-start.3
  7.2 2.3 copy-start.4
  7.2 2.3 copy-start.5
  16.0 1.9 copy-start.2
  24.2 100.6 %all-to-all-start.1 = ((bf16[8,4,128,512]{3,2,1,0:T(8,128)(2,1)}), bf16[8,4,128,512]{3,2,1,0:T(8,128)(2,1)}, u32[]{:S(2)}, u32[]{:S(2)}) async-start(bf16[8,4,128,512]{3,2,1,0:T(8,128)(2,1)} %bitcast.67), calls=%async_computation.1 | async-start | bytes 8388608 | tf_op jit(solution)/shard_map/all_to_all | solution.py:64
  124.8 102.0 %all-to-all-start = ((bf16[8,4,128,512]{3,2,1,0:T(8,128)(2,1)}), bf16[8,4,128,512]{3,2,1,0:T(8,128)(2,1)}, u32[]{:S(2)}, u32[]{:S(2)}) async-start(bf16[8,4,128,512]{3,2,1,0:T(8,128)(2,1)} %bitcast.65), calls=%async_computation | async-start | bytes 8388608 | tf_op jit(solution)/shard_map/all_to_all | solution.py:60
  129.4 197.5 %all-reduce.3.cloned.1.call-start = ((), (), s32[]{:S(2)}) async-start(), calls=%async_computation.3 | async-start | bytes 2097152 | tf_op jit(solution)/shard_map/psum | solution.py:11
  326.9 16.2 %copy-start = (f32[8,4,128,512]{3,2,1,0:T(8,128)S(1)}, f32[8,4,128,512]{3,2,1,0:T(8,128)}, u32[]{:S(2)}) copy-start(f32[8,4,128,512]{3,2,1,0:T(8,128)} %copy.60) | copy-start | bytes 25165828
  326.9 16.2 %copy-start.7 = (bf16[1024,512]{1,0:T(8,128)(2,1)S(1)}, bf16[1024,512]{1,0:T(8,128)(2,1)}, u32[]{:S(2)}) copy-start(bf16[1024,512]{1,0:T(8,128)(2,1)} %all-reduce.3.cloned.1.call-done) | copy-start | bytes 3145732
  343.1 10.8 %copy-start.1 = (f32[4,512,512]{2,1,0:T(8,128)S(1)}, f32[4,512,512]{2,1,0:T(8,128)}, u32[]{:S(2)}) copy-start(f32[4,512,512]{2,1,0:T(8,128)} %param.12) | copy-start | bytes 12582916
  365.5 98.6 %all-to-all-start.2 = ((bf16[8,513,512]{2,1,0:T(8,128)(2,1)}), bf16[8,513,512]{2,1,0:T(8,128)(2,1)}, u32[]{:S(2)}, u32[]{:S(2)}) async-start(bf16[8,513,512]{2,1,0:T(8,128)(2,1)} %pad_maximum_fusion), calls=%async_computation.2 | async-start | bytes 8519680 | tf_op jit(solution)/shard_map/all_to_all | solution.py:86
  370.1 60.0 %all-reduce.5.cloned.1.call-start = ((), (), s32[]{:S(2)}) async-start(), calls=%async_computation.4 | async-start | bytes 4194304 | tf_op jit(solution)/shard_map/psum | solution.py:76
  377.4 54.7 %copy-start.6 = (f32[4,512]{1,0:T(4,128)S(1)}, f32[4,512]{1,0:T(4,128)}, u32[]{:S(2)}) copy-start(f32[4,512]{1,0:T(4,128)} %param.13) | copy-start | bytes 24580
Sparse Core Ops, SparseCore 0:
  142.1 184.7 all-reduce.2
  377.6 52.4 all-reduce.4
where the time goes:
time: 499 us; the launch traced here: 491 us
  waiting for transfers between devices  333 us (67%)
  matrix products  77 us (15%)
  starting transfers between devices  27.6 us (6%)
  local copies, waits for them, and re-layouts  20.5 us (4%)
  other arithmetic  18 us (4%)
  between operations  15.3 us (3%)
    all_to_all x1, waiting for transfers between devices, per_device(): lax.all_to_all(tail_send, 'rel', split_axis=0, concat_axis=0, tiled=True)  87 us
    all_to_all x1, waiting for transfers between devices, per_device(): lax.all_to_all(held_rows, 'rel', split_axis=0, concat_axis=0, tiled=True)  84.8 us
    psum x1, waiting for transfers between devices, broadcast(): return lax.psum(jnp.where(mine, shard, jnp.zeros_like(shard)), axis)  82.8 us
    psum x1, waiting for transfers between devices, per_device(): lax.psum(partial_value.astype(jnp.bfloat16), 'grp').astype(jnp.float32)  52.6 us
    all_to_all x1, waiting for transfers between devices, per_device(): lax.all_to_all(packed, 'rel', split_axis=0, concat_axis=0, tiled=True)  25.8 us
    dot_general x3, matrix products, select_rows(): jnp.dot(selector, rows, preferred_element_type=jnp.float32)  22.5 us
    dot_general x1, matrix products, score_rows(): jnp.dot(query_rows, negatives.T, preferred_element_type=jnp.float32)  16.2 us
    psum x1, starting transfers between devices, broadcast(): return lax.psum(jnp.where(mine, shard, jnp.zeros_like(shard)), axis)  10.9 us
  transfers between devices with their start and end apart: 5, of which 5 were waited for; matrix products, arithmetic and copies ran while one was open for 8% of the time, Pallas kernels for 0%

commit v1 on v0

--- a/solution.py
+++ b/solution.py
@@ -61,7 +61,19 @@
     tail_send = select_rows(one_hot(slot_ids[:, 1], shard_rows), entities).reshape(
         layout + (width,)
     )
-    held_tails = lax.all_to_all(tail_send, "rel", split_axis=0, concat_axis=0, tiled=True)
+    ways, here = (lax.axis_size("rel"), lax.axis_index("rel"))
+    width_2 = tail_send.shape[0] // ways
+    dims = list(tail_send.shape)
+    dims[0] = width_2
+    height = dims[0]
+    dims[0] = height * ways
+    full = jnp.zeros(dims, tail_send.dtype)
+    for mask in range(ways):
+        part = lax.dynamic_slice_in_dim(tail_send, (here ^ mask) * width_2, width_2, axis=0)
+        if mask:
+            part = lax.ppermute(part, "rel", [(d, d ^ mask) for d in range(ways)])
+        full = lax.dynamic_update_slice_in_dim(full, part, (here ^ mask) * height, axis=0)
+    held_tails = full
     matrices = rel_weight.astype(jnp.bfloat16)
     projected = jnp.einsum(
         "srcd,rde->srce", held_rows, matrices, preferred_element_type=jnp.float32

time: 499 us -> 448 us (0.90)
  waiting for transfers between devices: 333 us -> 282 us
  local copies, waits for them, and re-layouts: 20.5 us -> 31.1 us
  other arithmetic: 18 us -> 12.3 us
    ppermute x0 -> x7, waiting for transfers between devices: none -> 138 us  [per_device(): part = lax.ppermute(part, 'rel', [(d, d ^ mask) for d in range(ways)])]
    all_to_all x1 -> x0, waiting for transfers between devices: 87 us -> none  [per_device(): lax.all_to_all(tail_send, 'rel', split_axis=0, concat_axis=0, tiled=True)]
    all_to_all x1, waiting for transfers between devices: 84.8 us -> 0.01 us  [per_device(): lax.all_to_all(held_rows, 'rel', split_axis=0, concat_axis=0, tiled=True)]
    psum x1, waiting for transfers between devices: 82.8 us -> 65.6 us  [broadcast(): return lax.psum(jnp.where(mine, shard, jnp.zeros_like(shard)), axis)]
    ppermute x0 -> x7, starting transfers between devices: none -> 13.3 us  [per_device(): part = lax.ppermute(part, 'rel', [(d, d ^ mask) for d in range(ways)])]
    psum x1, starting transfers between devices: 10.9 us -> 0.5 us  [broadcast(): return lax.psum(jnp.where(mine, shard, jnp.zeros_like(shard)), axis)]
    all_to_all x1 -> x0, starting transfers between devices: 7.31 us -> none  [per_device(): lax.all_to_all(tail_send, 'rel', split_axis=0, concat_axis=0, tiled=True)]
    dynamic_update_slice x0 -> x8, local copies, waits for them, and re-layouts: none -> 6.55 us  [per_device(): lax.dynamic_update_slice_in_dim(full, part, (here ^ mask) * height, axis=0)]
  transfers between devices with their start and end apart: 5 -> 11, of which waited for: 5 -> 8; matrix products, arithmetic and copies ran while one was open for 8% -> 10% of each run, Pallas kernels for 0% -> 0%
where the time goes in v1:
time: 448 us; the launch traced here: 442 us
  waiting for transfers between devices  282 us (63%)
  matrix products  75.2 us (17%)
  local copies, waits for them, and re-layouts  31.1 us (7%)
  starting transfers between devices  25.7 us (6%)
  between operations  15.3 us (3%)
  other arithmetic  12.3 us (3%)
    ppermute x7, waiting for transfers between devices, per_device(): part = lax.ppermute(part, 'rel', [(d, d ^ mask) for d in range(ways)])  138 us
    psum x1, waiting for transfers between devices, broadcast(): return lax.psum(jnp.where(mine, shard, jnp.zeros_like(shard)), axis)  65.6 us
    psum x1, waiting for transfers between devices, per_device(): lax.psum(partial_value.astype(jnp.bfloat16), 'grp').astype(jnp.float32)  52.8 us
    all_to_all x1, waiting for transfers between devices, per_device(): lax.all_to_all(packed, 'rel', split_axis=0, concat_axis=0, tiled=True)  25.8 us
    dot_general x3, matrix products, select_rows(): jnp.dot(selector, rows, preferred_element_type=jnp.float32)  21.9 us
    dot_general x1, matrix products, score_rows(): jnp.dot(query_rows, negatives.T, preferred_element_type=jnp.float32)  16.5 us
    ppermute x7, starting transfers between devices, per_device(): part = lax.ppermute(part, 'rel', [(d, d ^ mask) for d in range(ways)])  13.3 us
    dot_general x1, matrix products, score_rows(): jnp.dot(coefs, negatives, preferred_element_type=jnp.float32)  11.5 us
  transfers between devices with their start and end apart: 11, of which 8 were waited for; matrix products, arithmetic and copies ran while one was open for 10% of the time, Pallas kernels for 0%

profile of v1, /device:TPU:0, one launch (start us, length us, event | category | flops | bytes accessed | tf_op | source)
XLA Modules:
  0.0 442.1 jit_solution(15120559767810166360)
XLA Ops:
  7.2 2.3 fusion.29
  9.9 6.1 %scatter_custom_fusion = s32[4096,2]{1,0:T(8,128)S(1)} fusion(s32[2048]{0:T(1024)S(1)} %bitcast.94, s32[2048,2]{1,0:T(8,128)S(1)} %copy.84, s32[]{:T(128)} %constant.23.clone.1), kind=kCustom, calls=%fused_computation.46 | custom fusion | bytes 32772 | tf_op jit(solution)/shard_map/scatter | solution.py:56
  17.9 6.2 %fusion.14 = bf16[4096,512]{1,0:T(8,128)(2,1)} fusion(bf16[1024,512]{1,0:T(8,128)(2,1)S(1)} %copy-done.3, s32[4096]{0:T(1024)S(1)} %get-tuple-element.5), kind=kOutput, calls=%fused_computation.23 | convolution fusion | flops 4301258752 | bytes 5259264 | tf_op jit(solution)/shard_map/dot_general | solution.py:34
  24.1 7.3 %all-to-all-start = ((bf16[8,4,128,512]{3,2,1,0:T(8,128)(2,1)}), bf16[8,4,128,512]{3,2,1,0:T(8,128)(2,1)}, u32[]{:S(2)}, u32[]{:S(2)}) async-start(bf16[8,4,128,512]{3,2,1,0:T(8,128)(2,1)} %bitcast.82), calls=%async_computation | async-start | bytes 8388608 | tf_op jit(solution)/shard_map/all_to_all | solution.py:60
  32.0 5.6 %fusion.13 = bf16[4096,512]{1,0:T(8,128)(2,1)S(1)} fusion(bf16[1024,512]{1,0:T(8,128)(2,1)S(1)} %copy-done.3, s32[4096]{0:T(1024)S(1)} %get-tuple-element.4), kind=kOutput, calls=%fused_computation.22 | convolution fusion | flops 4301258752 | bytes 5259264 | tf_op jit(solution)/shard_map/dot_general | solution.py:34
  37.6 2.0 copy-done.1
  40.8 2.0 collective-permute-start
  44.3 2.9 collective-permute-start.3
  52.0 28.1 %collective-permute-done = bf16[1,4,128,512]{3,2,0,1:T(8,128)(2,1)} collective-permute-done((bf16[1,4,128,512]{3,2,0,1:T(8,128)(2,1)}, bf16[1,4,128,512]{3,2,0,1:T(8,128)(2,1)}, u32[]{:S(2)}, u32[]{:S(2)}) %collective-permute-start) | collective-permute-done | bytes 524320 | tf_op jit(solution)/shard_map/ppermute | solution.py:74
  82.9 34.5 %collective-permute-done.1 = bf16[1,4,128,512]{3,2,0,1:T(8,128)(2,1)} collective-permute-done((bf16[1,4,128,512]{3,2,0,1:T(8,128)(2,1)}, bf16[1,4,128,512]{3,2,0,1:T(8,128)(2,1)}, u32[]{:S(2)}, u32[]{:S(2)}) %collective-permute-start.1) | collective-permute-done | bytes 524320 | tf_op jit(solution)/shard_map/ppermute | solution.py:74
  117.5 3.7 collective-permute-start.6
  122.2 6.5 %collective-permute-done.2 = bf16[1,4,128,512]{3,2,0,1:T(8,128)(2,1)} collective-permute-done((bf16[1,4,128,512]{3,2,0,1:T(8,128)(2,1)}, bf16[1,4,128,512]{3,2,0,1:T(8,128)(2,1)}, u32[]{:S(2)}, u32[]{:S(2)}) %collective-permute-start.2) | collective-permute-done | bytes 524320 | tf_op jit(solution)/shard_map/ppermute | solution.py:74
  129.8 58.5 %collective-permute-done.3 = bf16[1,4,128,512]{3,2,0,1:T(8,128)(2,1)} collective-permute-done((bf16[1,4,128,512]{3,2,0,1:T(8,128)(2,1)S(1)}, bf16[1,4,128,512]{3,2,0,1:T(8,128)(2,1)}, u32[]{:S(2)}, u32[]{:S(2)}) %collective-permute-start.3) | collective-permute-done | bytes 524320 | tf_op jit(solution)/shard_map/ppermute | solution.py:74
  189.3 10.7 %collective-permute-done.4 = bf16[1,4,128,512]{3,2,0,1:T(8,128)(2,1)} collective-permute-done((bf16[1,4,128,512]{3,2,0,1:T(8,128)(2,1)S(1)}, bf16[1,4,128,512]{3,2,0,1:T(8,128)(2,1)}, u32[]{:S(2)}, u32[]{:S(2)}) %collective-permute-start.4) | collective-permute-done | bytes 524320 | tf_op jit(solution)/shard_map/ppermute | solution.py:74
  201.2 2.0 copy-done
  203.3 4.4 copy.95
  207.6 7.1 %multiply_reduce_fusion = (f32[8,4,128]{2,0,1:T(8,128)S(1)}, bf16[8,4,128,512]{3,2,0,1:T(8,128)(2,1)S(1)}) fusion(bf16[8,4,128,512]{3,2,0,1:T(8,128)(2,1)} %copy-done, f32[4,512,512]{2,1,0:T(8,128)} %param.12, bf16[8,4,128,512]{3,2,1,0:T(8,128)(2,1)} %all-to-all-done), kind=kOutput, calls=%fused_computation.18 | convolution fusion | flops 2159013888 | bytes 16793600 | tf_op jit(solution)/shard_map/srcd,rde->srce/dot_general | solution.py:78
  214.8 2.5 copy.96
  217.2 65.6 %all-reduce.3.cloned.1.call-done = bf16[1024,512]{1,0:T(8,128)(2,1)} async-done(((bf16[1024,512]{1,0:T(8,128)(2,1)}), bf16[1024,512]{1,0:T(8,128)(2,1)}) %all-reduce.3.cloned.1.call-update) | async-done | bytes 1048592 | tf_op jit(solution)/shard_map/psum | solution.py:11
  282.8 16.5 %fusion.2 = (f32[4096]{0:T(1024)S(1)}, f32[4096,1024]{0,1:T(8,128)}) fusion(bf16[4096,512]{1,0:T(8,128)(2,1)} %bitcast.83, bf16[1024,512]{1,0:T(8,128)(2,1)} %all-reduce.3.cloned.1.call-done), kind=kOutput, calls=%fused_computation.5 | convolution fusion | flops 4324323328 | bytes 22036480 | tf_op jit(solution)/shard_map/dot_general | solution.py:16
  299.4 11.5 %fusion.9 = bf16[4096,512]{1,0:T(8,128)(2,1)S(1)} fusion(f32[8,4,128,512]{3,2,1,0:T(8,128)} %copy.95, bf16[1024,512]{1,0:T(8,128)(2,1)S(1)} %copy-done.8, f32[4096,1024]{0,1:T(8,128)} %get-tuple-element.18, f32[4096]{0:T(1024)S(1)} %bitcast.86), kind=kOutput, calls=%fused_computation.17 | convolution fusion | flops 4322230272 | bytes 30425088 | tf_op jit(solution)/shard_map/dot_general | solution.py:20
  311.0 2.4 convert_bitcast_fusion
  313.8 2.3 pad_maximum_fusion
  316.1 4.5 %all-to-all-start.1 = ((bf16[8,513,512]{2,1,0:T(8,128)(2,1)}), bf16[8,513,512]{2,1,0:T(8,128)(2,1)}, u32[]{:S(2)}, u32[]{:S(2)}) async-start(bf16[8,513,512]{2,1,0:T(8,128)(2,1)} %pad_maximum_fusion), calls=%async_computation.1 | async-start | bytes 8519680 | tf_op jit(solution)/shard_map/all_to_all | solution.py:98
  320.7 7.2 %bitcast_convert_fusion = bf16[4,512,512]{2,1,0:T(8,128)(2,1)} fusion(bf16[8,4,128,512]{3,2,1,0:T(8,128)(2,1)} %all-to-all-done, bf16[8,4,128,512]{3,2,1,0:T(8,128)(2,1)} %bitcast.96), kind=kOutput, calls=%fused_computation.29 | convolution fusion | flops 2148532224 | bytes 10485760 | tf_op jit(solution)/shard_map/srcd,srce->rde/dot_general | solution.py:85
  327.9 52.8 %all-reduce.5.cloned.1.call-done = bf16[4,512,512]{2,1,0:T(8,128)(2,1)} async-done(((bf16[4,512,512]{2,1,0:T(8,128)(2,1)}), bf16[4,512,512]{2,1,0:T(8,128)(2,1)}) %all-reduce.5.cloned.1.call-update) | async-done | bytes 2097168 | tf_op jit(solution)/shard_map/psum | solution.py:88
  380.7 2.1 fusion.15
  383.4 5.5 %fusion.16 = f32[4,512,512]{2,1,0:T(8,128)} fusion(f32[4,512,512]{2,1,0:T(8,128)} %param.12, bf16[4,512,512]{2,1,0:T(8,128)(2,1)} %all-reduce.5.cloned.1.call-done, f32[4,512]{1,0:T(4,128)S(1)} %get-tuple-element.6), kind=kLoop, calls=%fused_computation.28 | loop fusion | flops 3145728 | bytes 10493952 | tf_op jit(solution)/shard_map/sub | solution.py:26
  388.9 25.8 %all-to-all-done.1 = bf16[8,513,512]{2,1,0:T(8,128)(2,1)} async-done(((bf16[8,513,512]{2,1,0:T(8,128)(2,1)}), bf16[8,513,512]{2,1,0:T(8,128)(2,1)}, u32[]{:S(2)}, u32[]{:S(2)}) %all-to-all-start.1) | async-done | bytes 4202528 | tf_op jit(solution)/shard_map/all_to_all | solution.py:98
  415.5 6.4 %fusion.1 = f32[1,2048]{1,0:T(1,128)S(1)} fusion(bf16[4096,1]{0,1:T(2,128)(2,1)S(1)} %bitcast.87, s32[2048]{0:T(1024)S(1)} %bitcast.92), kind=kOutput, calls=%fused_computation.4 | convolution fusion | flops 25165824 | bytes 24576 | tf_op jit(solution)/shard_map/dot_general | solution.py:104
  422.5 2.5 slice.19
  425.0 10.1 %fusion.21 = bf16[2048,512]{1,0:T(8,128)(2,1)} fusion(bf16[4096,512]{1,0:T(8,128)(2,1)S(1)} %bitcast.84, s32[2048]{0:T(1024)S(1)} %bitcast.93), kind=kOutput, calls=%fused_computation.36 | convolution fusion | flops 8599371776 | bytes 6299648 | tf_op jit(solution)/shard_map/dot_general | solution.py:34
  (56 shorter events, 19.5 us)
Async XLA Ops:
  7.2 2.3 copy-start.4
  7.2 2.3 copy-start.5
  7.2 2.3 copy-start.6
  16.0 1.9 copy-start.3
  24.1 183.5 %all-to-all-start = ((bf16[8,4,128,512]{3,2,1,0:T(8,128)(2,1)}), bf16[8,4,128,512]{3,2,1,0:T(8,128)(2,1)}, u32[]{:S(2)}, u32[]{:S(2)}) async-start(bf16[8,4,128,512]{3,2,1,0:T(8,128)(2,1)} %bitcast.82), calls=%async_computation | async-start | bytes 8388608 | tf_op jit(solution)/shard_map/all_to_all | solution.py:60
  31.5 251.4 %all-reduce.3.cloned.1.call-start = ((), (), s32[]{:S(2)}) async-start(), calls=%async_computation.2 | async-start | bytes 2097152 | tf_op jit(solution)/shard_map/psum | solution.py:11
  37.6 2.0 copy-start.1
  40.8 39.2 %collective-permute-start = (bf16[1,4,128,512]{3,2,0,1:T(8,128)(2,1)}, bf16[1,4,128,512]{3,2,0,1:T(8,128)(2,1)}, u32[]{:S(2)}, u32[]{:S(2)}) collective-permute-start(bf16[1,4,128,512]{3,2,0,1:T(8,128)(2,1)} %get-tuple-element.16), channel_id=1, source_target_pairs={{0,1},{1,0},{2,3},{3,2},{4,5},{5,4},{6,7},{7,6},{8,9},{9,8},{10,11... | collective-permute-start | bytes 1572872 | tf_op jit(solution)/shard_map/ppermute | solution.py:74
  42.8 74.6 %collective-permute-start.1 = (bf16[1,4,128,512]{3,2,0,1:T(8,128)(2,1)}, bf16[1,4,128,512]{3,2,0,1:T(8,128)(2,1)}, u32[]{:S(2)}, u32[]{:S(2)}) collective-permute-start(bf16[1,4,128,512]{3,2,0,1:T(8,128)(2,1)} %get-tuple-element.15), channel_id=1, source_target_pairs={{0,2},{1,3},{2,0},{3,1},{4,6},{5,7},{6,4},{7,5},{8,10},{9,11},{10,... | collective-permute-start | bytes 1572872 | tf_op jit(solution)/shard_map/ppermute | solution.py:74
  44.3 84.4 %collective-permute-start.2 = (bf16[1,4,128,512]{3,2,0,1:T(8,128)(2,1)}, bf16[1,4,128,512]{3,2,0,1:T(8,128)(2,1)}, u32[]{:S(2)}, u32[]{:S(2)}) collective-permute-start(bf16[1,4,128,512]{3,2,0,1:T(8,128)(2,1)} %get-tuple-element.14), channel_id=1, source_target_pairs={{0,3},{1,2},{2,1},{3,0},{4,7},{5,6},{6,5},{7,4},{8,11},{9,10},{10,... | collective-permute-start | bytes 1572872 | tf_op jit(solution)/shard_map/ppermute | solution.py:74
  44.3 143.9 %collective-permute-start.3 = (bf16[1,4,128,512]{3,2,0,1:T(8,128)(2,1)S(1)}, bf16[1,4,128,512]{3,2,0,1:T(8,128)(2,1)}, u32[]{:S(2)}, u32[]{:S(2)}) collective-permute-start(bf16[1,4,128,512]{3,2,0,1:T(8,128)(2,1)S(1)} %get-tuple-element.13), channel_id=1, source_target_pairs={{0,4},{1,5},{2,6},{3,7},{4,0},{5,1},{6,2},{7,3},{8,12},{9,13},{10,... | collective-permute-start | bytes 1572872 | tf_op jit(solution)/shard_map/ppermute | solution.py:74
  47.2 152.8 %collective-permute-start.4 = (bf16[1,4,128,512]{3,2,0,1:T(8,128)(2,1)S(1)}, bf16[1,4,128,512]{3,2,0,1:T(8,128)(2,1)}, u32[]{:S(2)}, u32[]{:S(2)}) collective-permute-start(bf16[1,4,128,512]{3,2,0,1:T(8,128)(2,1)S(1)} %get-tuple-element.12), channel_id=1, source_target_pairs={{0,5},{1,4},{2,7},{3,6},{4,1},{5,0},{6,3},{7,2},{8,13},{9,12},{10,... | collective-permute-start | bytes 1572872 | tf_op jit(solution)/shard_map/ppermute | solution.py:74
  80.1 121.0 %collective-permute-start.5 = (bf16[1,4,128,512]{3,2,0,1:T(8,128)(2,1)S(1)}, bf16[1,4,128,512]{3,2,0,1:T(8,128)(2,1)S(1)}, u32[]{:S(2)}, u32[]{:S(2)}) collective-permute-start(bf16[1,4,128,512]{3,2,0,1:T(8,128)(2,1)S(1)} %get-tuple-element.11), channel_id=1, source_target_pairs={{0,6},{1,7},{2,4},{3,5},{4,2},{5,3},{6,0},{7,1},{8,14},{9,15},{10,... | collective-permute-start | bytes 1572872 | tf_op jit(solution)/shard_map/ppermute | solution.py:74
  117.5 83.7 %collective-permute-start.6 = (bf16[1,4,128,512]{3,2,0,1:T(8,128)(2,1)S(1)}, bf16[1,4,128,512]{3,2,0,1:T(8,128)(2,1)S(1)}, u32[]{:S(2)}, u32[]{:S(2)}) collective-permute-start(bf16[1,4,128,512]{3,2,0,1:T(8,128)(2,1)S(1)} %get-tuple-element.10), channel_id=1, source_target_pairs={{0,7},{1,6},{2,5},{3,4},{4,3},{5,2},{6,1},{7,0},{8,15},{9,14},{10,... | collective-permute-start | bytes 1572872 | tf_op jit(solution)/shard_map/ppermute | solution.py:74
  201.2 2.0 copy-start
  282.8 16.6 %copy-start.8 = (bf16[1024,512]{1,0:T(8,128)(2,1)S(1)}, bf16[1024,512]{1,0:T(8,128)(2,1)}, u32[]{:S(2)}) copy-start(bf16[1024,512]{1,0:T(8,128)(2,1)} %all-reduce.3.cloned.1.call-done) | copy-start | bytes 3145732
  299.4 11.5 %copy-start.2 = (f32[4,512,512]{2,1,0:T(8,128)S(1)}, f32[4,512,512]{2,1,0:T(8,128)}, u32[]{:S(2)}) copy-start(f32[4,512,512]{2,1,0:T(8,128)} %param.12) | copy-start | bytes 12582916
  310.9 2.4 copy-start.9
  316.1 98.5 %all-to-all-start.1 = ((bf16[8,513,512]{2,1,0:T(8,128)(2,1)}), bf16[8,513,512]{2,1,0:T(8,128)(2,1)}, u32[]{:S(2)}, u32[]{:S(2)}) async-start(bf16[8,513,512]{2,1,0:T(8,128)(2,1)} %pad_maximum_fusion), calls=%async_computation.1 | async-start | bytes 8519680 | tf_op jit(solution)/shard_map/all_to_all | solution.py:98
  320.6 60.0 %all-reduce.5.cloned.1.call-start = ((), (), s32[]{:S(2)}) async-start(), calls=%async_computation.3 | async-start | bytes 4194304 | tf_op jit(solution)/shard_map/psum | solution.py:88
  327.9 54.9 %copy-start.7 = (f32[4,512]{1,0:T(4,128)S(1)}, f32[4,512]{1,0:T(4,128)}, u32[]{:S(2)}) copy-start(f32[4,512]{1,0:T(4,128)} %param.13) | copy-start | bytes 24580
Sparse Core Ops, SparseCore 0:
  50.5 232.2 all-reduce.2
  328.0 52.6 all-reduce.4
